TPU v7x, 512 devices: a whole 4x8x8 slice. The times are simulated.
512 devices in a mesh: exp: 128 (over y, z, core), hid: 4 (over x).
Axes of the slice: x: 4, y: 8, z: 8, core: 2. Of those that a mesh axis runs over, the one named last changes fastest.
Arguments:
- tokens: bfloat16 [4096, 4096], P('exp', 'hid'), may hold values from -6 to 6
- expert_ids: int32 [4096, 8], P('exp'), may hold values from 0 to 127, all different within a row; in each aligned block of 16 rows (0 to 15, 16 to 31, ...) at most 2 rows name the same one
- combine: float32 [4096, 8], P('exp'), may hold values from 0.05 to 0.4
- sign_bits: int32 [128, 768], P('exp'), may hold values from 0 to 1
- w_gate: bfloat16 [128, 768, 4096], P('exp', 'hid'), may hold values from -0.09375 to 0.09375
- w_up: bfloat16 [128, 768, 4096], P('exp', 'hid'), may hold values from -0.09375 to 0.09375
- w_down: bfloat16 [128, 768, 4096], P('exp', 'hid'), may hold values from -0.21875 to 0.21875
Outputs:
- next_input: bfloat16 [4096, 4096], P('exp', 'hid')
- hessian: bfloat16 [128, 768, 768], P('exp', 'hid')
Inputs may be any that keep to these rules, and one draw needn't show every extreme that they name: `expert_ids`: each row names 8 different experts. Within each aligned block of 16 rows (one micro-batch of one index of exp) no expert is named by more than 2 rows, a bound that some block reaches. `sign_bits`: 0 stands for the sign -1, 1 for +1.
All inputs are finite; a program needn't handle non-finite values.
Results may differ from a plain program's by a relative error of at most 0.0065.
Values may be sent and summed in bfloat16 or wider, within the bound.
No kernel may reach another device: no remote copies, remote signals or barrier semaphores. Data moves between devices by JAX's collectives and lax.ppermute only.
A program may use at most 64 MiB of HBM per device.

v0:
```python
import jax
import jax.numpy as jnp
import numpy as np
from jax import lax
from jax.sharding import PartitionSpec as P


def paley_twelve():
    residues = set((number * number % 11 for number in range(1, 11)))
    legendre = [0] + [1 if number in residues else -1 for number in range(1, 11)]
    hadamard = np.zeros((12, 12))
    hadamard[0, 1:] = 1.0
    hadamard[1:, 0] = -1.0
    for row_index in range(11):
        for col_index in range(11):
            hadamard[row_index + 1, col_index + 1] = legendre[(col_index - row_index) % 11]
    return hadamard + np.eye(12)


def sylvester(order_size):
    positions = jnp.arange(order_size, dtype=jnp.int32)
    common = positions[:, None] & positions[None, :]
    parity = jnp.zeros_like(common)
    for bit_pos in range(order_size.bit_length()):
        parity = parity + (common >> bit_pos & 1)
    return (1 - 2 * (parity % 2)).astype(jnp.float32)


def rotate(hidden, sign_rows, paley_table, sylvester_table):
    values = hidden.astype(jnp.float32) * jnp.expand_dims(sign_rows, -2)
    blocks = values.reshape(values.shape[:-1] + (12, sylvester_table.shape[0]))
    turned = jnp.einsum(
        "...ab,ca,db->...cd", blocks, paley_table, sylvester_table, precision=lax.Precision.HIGHEST
    )
    return turned.reshape(values.shape)


def rank_of_pick(ids_block, experts):
    flat_ids = ids_block.reshape(-1)
    onehot = (flat_ids[:, None] == jnp.arange(experts, dtype=jnp.int32)[None, :]).astype(jnp.int32)
    before = jnp.cumsum(onehot, axis=0) - onehot
    return jnp.sum(before * onehot, axis=1).reshape(ids_block.shape)


def local(tokens, expert_ids, combine, sign_bits, w_gate, w_up, w_down):
    n_exp = lax.axis_size("exp")
    n_hid = lax.axis_size("hid")
    hid_index = lax.axis_index("hid")
    local_experts = w_gate.shape[0]
    experts = local_experts * n_exp
    tok_rows = tokens.shape[0]
    half_rows = tok_rows // 2
    top_count = expert_ids.shape[1]
    capacity = min(half_rows, max(2, 2 * half_rows * top_count // experts))
    hidden_units = sign_bits.shape[1]
    share_rows = hidden_units // n_hid
    slot_count = n_exp * capacity
    paley_table = jnp.asarray(paley_twelve(), jnp.float32)
    sylvester_table = sylvester(hidden_units // 12)
    sign_rows = (2 * sign_bits - 1).astype(jnp.float32)
    gram_scale = experts / (tok_rows * n_exp * top_count * hidden_units)
    down_cols = lax.all_to_all(w_down, "hid", split_axis=2, concat_axis=1, tiled=True)
    gram_total = jnp.zeros((local_experts, share_rows, hidden_units), jnp.float32)
    results = []
    for batch_index in range(2):
        first_row = batch_index * half_rows
        ids_block = expert_ids[first_row : first_row + half_rows]
        picks_rank = rank_of_pick(ids_block, experts)
        target = ids_block * capacity + picks_rank
        selector = jnp.any(
            target[None, :, :] == jnp.arange(experts * capacity, dtype=jnp.int32)[:, None, None],
            axis=2,
        ).astype(jnp.bfloat16)
        sending = jnp.dot(
            selector, tokens[first_row : first_row + half_rows], preferred_element_type=jnp.float32
        ).astype(jnp.bfloat16)
        arrived = lax.all_to_all(sending, "exp", split_axis=0, concat_axis=0, tiled=True)
        arrived = lax.all_gather(arrived, "hid", axis=1, tiled=True)
        row_width = arrived.shape[1]
        expert_in = arrived.reshape(n_exp, local_experts, capacity, row_width).transpose(1, 0, 2, 3)
        expert_in = expert_in.reshape(local_experts, slot_count, row_width)
        gate_act = jnp.einsum("esd,efd->esf", expert_in, w_gate, preferred_element_type=jnp.float32)
        up_act = jnp.einsum("esd,efd->esf", expert_in, w_up, preferred_element_type=jnp.float32)
        hidden = (jax.nn.silu(gate_act) * up_act).astype(jnp.bfloat16)
        full_hidden = lax.all_gather(hidden, "hid", axis=2, tiled=True)
        summed = jnp.einsum(
            "esf,efd->esd", full_hidden, down_cols, preferred_element_type=jnp.float32
        ).astype(jnp.bfloat16)
        outgoing = summed.reshape(local_experts, n_exp, capacity, -1).transpose(1, 0, 2, 3)
        outgoing = outgoing.reshape(n_exp * local_experts * capacity, -1)
        back_rows = lax.all_to_all(outgoing, "exp", split_axis=0, concat_axis=0, tiled=True)
        picked = back_rows[target]
        weights = combine[first_row : first_row + half_rows]
        mixed_rows = tokens[first_row : first_row + half_rows].astype(jnp.float32) + jnp.sum(
            weights[:, :, None] * picked.astype(jnp.float32), axis=1
        )
        results.append(mixed_rows.astype(jnp.bfloat16))
        rotated = rotate(full_hidden, sign_rows, paley_table, sylvester_table)
        own_rotated = lax.dynamic_slice_in_dim(rotated, hid_index * share_rows, share_rows, 2)
        gram_total = gram_total + jnp.einsum(
            "esi,esj->eij", own_rotated, rotated, precision=lax.Precision.HIGHEST
        )
    hessian = (gram_total * gram_scale).astype(jnp.bfloat16)
    return (jnp.concatenate(results, axis=0), hessian)


def solution(mesh):
    placed = (
        P("exp", "hid"),
        P("exp", None),
        P("exp", None),
        P("exp", None),
        P("exp", "hid", None),
        P("exp", "hid", None),
        P("exp", "hid", None),
    )
    return jax.shard_map(
        local,
        mesh=mesh,
        in_specs=placed,
        out_specs=(P("exp", "hid"), P("exp", "hid", None)),
        check_vma=False,
    )
```

profile of v0, /device:TPU:1, one launch (start us, length us, event | category | flops | bytes accessed | tf_op | source)
XLA Modules:
  0.0 254.6 jit_solution(8127304555894847153)
XLA Ops:
  7.2 0.9 fusion.82
  8.1 0.1 copy.50
  8.2 0.1 eq.65
  8.3 0.1 fusion.40
  8.4 0.2 reduce_window_sum.18
  8.5 0.2 select_reduce_fusion
  8.7 0.1 reshape.129
  8.8 0.1 fusion.39
  9.0 1.1 convolution_convert_fusion.1
  10.1 0.2 all_to_all.52
  10.3 37.8 %all_to_all.63 = bf16[128,2,1024]{2,1,0:T(2,128)(2,1)S(1)} all-to-all(bf16[128,2,1024]{2,1,0:T(2,128)(2,1)S(1)} %all_to_all.52), channel_id=1, replica_groups=mesh['exp'=128,'hid'=4] {'exp'}, dimensions={0} | all-to-all | bytes 1048576 | tf_op jit(solution)/shard_map/all_to_all | solution.py:77
  48.0 1.0 all_to_all.54
  49.2 0.1 eq.58
  49.3 0.1 fusion.41
  49.4 0.2 reduce_window_sum.17
  49.5 0.2 select_reduce_fusion.1
  49.7 0.1 reshape.124
  49.8 0.1 fusion.38
  50.0 0.3 convolution_convert_fusion.3
  50.3 0.2 all_to_all.43
  50.5 26.2 %all_to_all.64 = bf16[128,2,1024]{2,1,0:T(2,128)(2,1)S(1)} all-to-all(bf16[128,2,1024]{2,1,0:T(2,128)(2,1)S(1)} %all_to_all.43), channel_id=1, replica_groups=mesh['exp'=128,'hid'=4] {'exp'}, dimensions={0} | all-to-all | bytes 1048576 | tf_op jit(solution)/shard_map/all_to_all | solution.py:77
  76.7 1.0 all_to_all.45
  77.7 9.9 %copy.40 = bf16[1,192,4096]{1,0,2:T(2,128)(2,1)} copy(bf16[1,192,4096]{2,1,0:T(8,128)(2,1)} %param.14) | data formatting | bytes 3145728 | tf_op args[6]
  87.6 0.5 broadcast.82
  88.1 25.0 %reduce.2 = bf16[4096,192]{1,0:T(8,128)(2,1)} reduce(bf16[4096,1,192]{2,1,0:T(2,128)(2,1)} %bitcast.77, bf16[]{:T(256)} %broadcast.82), dimensions={1}, to_apply=%bitcast.61.reduce_sub_computation | reduce | bytes 3145730
  113.1 5.0 %reshape.170 = bf16[4,2,98304]{2,1,0:T(2,128)(2,1)} reshape(bf16[4096,192]{1,0:T(8,128)(2,1)} %reduce.2) | data formatting | bytes 3145728
  118.1 4.1 %all-to-all-start.1 = ((bf16[4,2,98304]{2,1,0:T(2,128)(2,1)}), bf16[4,2,98304]{2,1,0:T(2,128)(2,1)S(1)}, u32[]{:S(2)}, u32[]{:S(2)}) async-start(bf16[4,2,98304]{2,1,0:T(2,128)(2,1)} %reshape.170), calls=%async_computation.1 | async-start | bytes 3145728 | tf_op jit(solution)/shard_map/all_to_all | solution.py:62
  122.3 0.1 reshape.149
  122.4 0.7 copy.43
  123.1 0.1 reshape.141
  123.2 0.7 copy.38
  123.9 0.6 convert_reduce_fusion
  124.5 16.4 %all-to-all-done.1 = bf16[4,2,98304]{2,1,0:T(2,128)(2,1)S(1)} async-done(((bf16[4,2,98304]{2,1,0:T(2,128)(2,1)}), bf16[4,2,98304]{2,1,0:T(2,128)(2,1)S(1)}, u32[]{:S(2)}, u32[]{:S(2)}) %all-to-all-start.1) | async-done | bytes 1572896 | tf_op jit(solution)/shard_map/all_to_all | solution.py:62
  140.9 4.1 %reshape.171 = bf16[4096,1,192]{2,1,0:T(2,128)(2,1)} reshape(bf16[4,2,98304]{2,1,0:T(2,128)(2,1)S(1)} %all-to-all-done.1) | data formatting | bytes 3145728
  145.0 9.6 %copy.41 = bf16[1,192,4096]{2,1,0:T(8,128)(2,1)} copy(bf16[1,192,4096]{1,0,2:T(2,128)(2,1)} %bitcast.78) | data formatting | bytes 3145728 | tf_op jit(solution)/shard_map/all_to_all | solution.py:62
  154.6 2.9 %all_to_all.47 = bf16[1,192,4,1024]{3,2,1,0:T(4,128)(2,1)S(1)} reshape(bf16[1,192,4096]{2,1,0:T(8,128)(2,1)} %copy.41) | data formatting | bytes 3145728 | tf_op jit(solution)/shard_map/all_to_all | solution.py:62
  157.5 1.6 copy.42
  159.1 2.6 %fusion.4 = f32[256,192]{0,1:T(8,128)S(1)} fusion(bf16[256,4096]{1,0:T(8,128)(2,1)} %all-gather.7.cloned.1.call-done, bf16[1,192,4096]{2,1,0:T(8,128)(2,1)S(1)} %copy-done), kind=kOutput, calls=%fused_computation.6 | convolution fusion | flops 402653184 | bytes 3866624 | tf_op jit(solution)/shard_map/esd,efd->esf/dot_general | solution.py:82
  161.8 0.9 fusion.17
  162.7 9.6 %all-gather.1 = bf16[256,768]{0,1:T(8,128)(2,1)S(1)} all-gather(bf16[256,192]{0,1:T(8,128)(2,1)S(1)} %fusion.17), channel_id=3, replica_groups=mesh['exp'=128,'hid'=4] {'hid'}, dimensions={1}, use_global_device_ids=true | all-gather | bytes 491520 | tf_op jit(solution)/shard_map/all_gather | solution.py:85
  172.3 1.4 convolution_convert_fusion
  173.7 2.0 all_to_all.55
  175.7 12.7 %all-to-all-start.4 = ((bf16[128,2,1024]{2,1,0:T(2,128)(2,1)}), bf16[128,2,1024]{2,1,0:T(2,128)(2,1)}, u32[]{:S(2)}, u32[]{:S(2)}) async-start(bf16[128,2,1024]{2,1,0:T(2,128)(2,1)} %all_to_all.55), calls=%async_computation.4 | async-start | bytes 1048576 | tf_op jit(solution)/shard_map/all_to_all | solution.py:91
  188.5 2.6 %fusion.6 = f32[256,192]{0,1:T(8,128)S(1)} fusion(bf16[256,4096]{1,0:T(8,128)(2,1)} %all-gather.5.cloned.1.call-done, bf16[1,192,4096]{2,1,0:T(8,128)(2,1)S(1)} %copy-done), kind=kOutput, calls=%fused_computation.8 | convolution fusion | flops 402653184 | bytes 3866624 | tf_op jit(solution)/shard_map/esd,efd->esf/dot_general | solution.py:82
  191.1 0.8 fusion.20
  192.0 10.8 %all-gather = bf16[256,768]{0,1:T(8,128)(2,1)S(1)} all-gather(bf16[256,192]{0,1:T(8,128)(2,1)S(1)} %fusion.20), channel_id=2, replica_groups=mesh['exp'=128,'hid'=4] {'hid'}, dimensions={1}, use_global_device_ids=true | all-gather | bytes 491520 | tf_op jit(solution)/shard_map/all_gather | solution.py:85
  202.8 0.7 copy-done.4
  203.6 1.4 convolution_convert_fusion.2
  205.0 2.1 all_to_all.49
  207.0 1.2 convert_multiply_fusion
  208.2 1.4 fusion.25
  209.6 15.9 %all-to-all-start.2 = ((bf16[128,2,1024]{2,1,0:T(2,128)(2,1)}), bf16[128,2,1024]{2,1,0:T(2,128)(2,1)}, u32[]{:S(2)}, u32[]{:S(2)}) async-start(bf16[128,2,1024]{2,1,0:T(2,128)(2,1)} %all_to_all.49), calls=%async_computation.2 | async-start | bytes 1048576 | tf_op jit(solution)/shard_map/all_to_all | solution.py:91
  225.5 1.3 fusion.29
  226.8 0.9 fusion.34
  227.8 1.4 fusion.23
  229.2 1.3 fusion.27
  230.5 1.7 fusion.10
  232.1 1.2 all_to_all.57
  233.4 0.9 gather_fusion.1
  234.3 10.3 %all-to-all-done.2 = bf16[128,2,1024]{2,1,0:T(2,128)(2,1)} async-done(((bf16[128,2,1024]{2,1,0:T(2,128)(2,1)}), bf16[128,2,1024]{2,1,0:T(2,128)(2,1)}, u32[]{:S(2)}, u32[]{:S(2)}) %all-to-all-start.2) | async-done | bytes 524320 | tf_op jit(solution)/shard_map/all_to_all | solution.py:91
  244.6 1.2 all_to_all.51
  245.8 0.9 gather_fusion
  246.7 0.4 fusion.31
  247.1 0.6 pad_maximum_fusion
  (41 shorter events, 0.5 us)
Async XLA Ops:
  7.2 152.0 %copy-start = (bf16[1,192,4096]{2,1,0:T(8,128)(2,1)S(1)}, bf16[1,192,4096]{2,1,0:T(8,128)(2,1)}, u32[]{:S(2)}) copy-start(bf16[1,192,4096]{2,1,0:T(8,128)(2,1)} %param.12) | copy-start | bytes 4718596
  7.2 151.9 %all-gather.7.cloned.1.call-start = ((), (), s32[]{:S(2)}) async-start(), calls=%async_computation.6 | async-start | bytes 2621440 | tf_op jit(solution)/shard_map/all_gather | solution.py:78
  10.3 39.7 %copy-start.5 = (bf16[32,1024]{1,0:T(8,128)(2,1)S(1)}, bf16[32,1024]{1,0:T(8,128)(2,1)}, u32[]{:S(2)}) copy-start(bf16[32,1024]{1,0:T(8,128)(2,1)} %param.8) | copy-start | bytes 196612
  49.1 139.4 %all-gather.5.cloned.1.call-start = ((), (), s32[]{:S(2)}) async-start(), calls=%async_computation.5 | async-start | bytes 2621440 | tf_op jit(solution)/shard_map/all_gather | solution.py:78
  118.1 4.2 %copy-start.10 = (f32[32,8]{0,1:T(8,128)S(1)}, f32[32,8]{0,1:T(8,128)}, u32[]{:S(2)}) copy-start(f32[32,8]{0,1:T(8,128)} %param.10) | copy-start | bytes 3076
  118.1 5.8 %copy-start.11 = (s32[1,768]{1,0:T(1,128)S(1)}, s32[1,768]{1,0:T(1,128)}, u32[]{:S(2)}) copy-start(s32[1,768]{1,0:T(1,128)} %param.11) | copy-start | bytes 9220
  118.1 22.8 %all-to-all-start.1 = ((bf16[4,2,98304]{2,1,0:T(2,128)(2,1)}), bf16[4,2,98304]{2,1,0:T(2,128)(2,1)S(1)}, u32[]{:S(2)}, u32[]{:S(2)}) async-start(bf16[4,2,98304]{2,1,0:T(2,128)(2,1)} %reshape.170), calls=%async_computation.1 | async-start | bytes 3145728 | tf_op jit(solution)/shard_map/all_to_all | solution.py:62
  159.1 2.6 %copy-start.1 = (bf16[256,4096]{1,0:T(8,128)(2,1)S(1)}, bf16[256,4096]{1,0:T(8,128)(2,1)}, u32[]{:S(2)}) copy-start(bf16[256,4096]{1,0:T(8,128)(2,1)} %all-gather.7.cloned.1.call-done) | copy-start | bytes 6291460
  159.1 2.7 %copy-start.12 = (bf16[1,192,4096]{2,1,0:T(8,128)(2,1)S(1)}, bf16[1,192,4096]{2,1,0:T(8,128)(2,1)}, u32[]{:S(2)}) copy-start(bf16[1,192,4096]{2,1,0:T(8,128)(2,1)} %param.13) | copy-start | bytes 4718596
  161.8 10.5 %copy-start.3 = (bf16[1,4,192,1024]{3,2,1,0:T(8,128)(2,1)S(1)}, bf16[1,4,192,1024]{3,2,1,0:T(8,128)(2,1)}, u32[]{:S(2)}) copy-start(bf16[1,4,192,1024]{3,2,1,0:T(8,128)(2,1)} %copy.42) | copy-start | bytes 4718596
  175.7 33.9 %all-to-all-start.4 = ((bf16[128,2,1024]{2,1,0:T(2,128)(2,1)}), bf16[128,2,1024]{2,1,0:T(2,128)(2,1)}, u32[]{:S(2)}, u32[]{:S(2)}) async-start(bf16[128,2,1024]{2,1,0:T(2,128)(2,1)} %all_to_all.55), calls=%async_computation.4 | async-start | bytes 1048576 | tf_op jit(solution)/shard_map/all_to_all | solution.py:91
  188.5 2.6 %copy-start.2 = (bf16[256,4096]{1,0:T(8,128)(2,1)S(1)}, bf16[256,4096]{1,0:T(8,128)(2,1)}, u32[]{:S(2)}) copy-start(bf16[256,4096]{1,0:T(8,128)(2,1)} %all-gather.5.cloned.1.call-done) | copy-start | bytes 6291460
  188.5 2.7 %copy-start.13 = (bf16[1,192,4096]{2,1,0:T(8,128)(2,1)S(1)}, bf16[1,192,4096]{2,1,0:T(8,128)(2,1)}, u32[]{:S(2)}) copy-start(bf16[1,192,4096]{2,1,0:T(8,128)(2,1)} %param.13) | copy-start | bytes 4718596
  202.8 0.7 copy-start.4
  204.9 3.3 %copy-start.7 = (f32[12,12,1]{1,0,2:T(8,128)S(1)}, f32[12,12,1]{1,0,2:T(8,128)}, u32[]{:S(2)}) copy-start(f32[12,12,1]{1,0,2:T(8,128)} %constant.69) | copy-start | bytes 1732
  209.6 35.0 %all-to-all-start.2 = ((bf16[128,2,1024]{2,1,0:T(2,128)(2,1)}), bf16[128,2,1024]{2,1,0:T(2,128)(2,1)}, u32[]{:S(2)}, u32[]{:S(2)}) async-start(bf16[128,2,1024]{2,1,0:T(2,128)(2,1)} %all_to_all.49), calls=%async_computation.2 | async-start | bytes 1048576 | tf_op jit(solution)/shard_map/all_to_all | solution.py:91
  234.2 12.4 %copy-start.8 = (f32[16,8]{1,0:T(8,128)S(1)}, f32[16,8]{1,0:T(8,128)}, u32[]{:S(2)}) copy-start(f32[16,8]{1,0:T(8,128)} %copy.43) | copy-start | bytes 1540
  234.3 12.4 %copy-start.9 = (f32[16,8]{1,0:T(8,128)S(1)}, f32[16,8]{1,0:T(8,128)}, u32[]{:S(2)}) copy-start(f32[16,8]{1,0:T(8,128)} %copy.38) | copy-start | bytes 1540
  245.8 1.3 copy-start.6
Sparse Core Ops, SparseCore 0:
  49.2 29.5 all-gather.6
  80.8 36.1 all-gather.4
where the time goes:
time: 256 us; the launch traced here: 255 us
  blocking collectives  84.4 us (33%)
  local copies, waits for them, and re-layouts  48.2 us (19%)
  starting transfers between devices  32.8 us (13%)
  other arithmetic  29 us (11%)
  waiting for transfers between devices  26.7 us (10%)
  matrix products  19.1 us (7%)
  between operations  14.4 us (6%)
    all_to_all x2, blocking collectives, local(): lax.all_to_all(sending, 'exp', split_axis=0, concat_axis=0, tiled=True)  63.9 us
    all_to_all x2, starting transfers between devices, local(): lax.all_to_all(outgoing, 'exp', split_axis=0, concat_axis=0, tiled=True)  28.6 us
    unnamed x1, other arithmetic  25 us
    unnamed x34, local copies, waits for them, and re-layouts  20.6 us
    all_gather x2, blocking collectives, local(): full_hidden = lax.all_gather(hidden, 'hid', axis=2, tiled=True)  20.5 us
    all_to_all x1, waiting for transfers between devices, local(): lax.all_to_all(w_down, 'hid', split_axis=2, concat_axis=1, tiled=True)  16.4 us
    all_to_all x3, local copies, waits for them, and re-layouts, local(): lax.all_to_all(w_down, 'hid', split_axis=2, concat_axis=1, tiled=True)  14.1 us
    all_to_all x2, waiting for transfers between devices, local(): lax.all_to_all(outgoing, 'exp', split_axis=0, concat_axis=0, tiled=True)  10.3 us
  transfers between devices with their start and end apart: 5, of which 2 were waited for; matrix products, arithmetic and copies ran while one was open for 31% of the time, Pallas kernels for 0%

commit v1 on v0

--- a/solution.py
+++ b/solution.py
@@ -59,7 +59,10 @@
     sylvester_table = sylvester(hidden_units // 12)
     sign_rows = (2 * sign_bits - 1).astype(jnp.float32)
     gram_scale = experts / (tok_rows * n_exp * top_count * hidden_units)
-    down_cols = lax.all_to_all(w_down, "hid", split_axis=2, concat_axis=1, tiled=True)
+    down_cols = jnp.concatenate(
+        lax.all_to_all(jnp.stack(jnp.split(w_down, lax.axis_size("hid"), axis=2)), "hid", 0, 0),
+        axis=1,
+    )
     gram_total = jnp.zeros((local_experts, share_rows, hidden_units), jnp.float32)
     results = []
     for batch_index in range(2):

time: 256 us -> 200 us (0.78)
  local copies, waits for them, and re-layouts: 48.2 us -> 16.1 us
  other arithmetic: 29 us -> 5.34 us
  waiting for transfers between devices: 26.7 us -> 10.4 us
  blocking collectives: 84.4 us -> 98.2 us
  starting transfers between devices: 32.8 us -> 35.8 us
    unnamed x1 -> x0, other arithmetic: 25 us -> none
    unnamed x34 -> x28, local copies, waits for them, and re-layouts: 20.6 us -> 1.06 us
    all_to_all x1, waiting for transfers between devices: 16.4 us -> 0.01 us  [local(): lax.all_to_all(jnp.stack(jnp.split(w_down, lax.axis_size('hid'), axis=2))...]
    all_to_all x3 -> x0, local copies, waits for them, and re-layouts: 14.1 us -> none  [local(): lax.all_to_all(w_down, 'hid', split_axis=2, concat_axis=1, tiled=True)]
    all_gather x2, blocking collectives: 20.5 us -> 34.3 us  [local(): full_hidden = lax.all_gather(hidden, 'hid', axis=2, tiled=True)]
    all_to_all x2, starting transfers between devices: 28.6 us -> 31.6 us  [local(): lax.all_to_all(outgoing, 'exp', split_axis=0, concat_axis=0, tiled=True)]
  transfers between devices with their start and end apart: 5 -> 5, of which waited for: 2 -> 1; matrix products, arithmetic and copies ran while one was open for 31% -> 13% of each run, Pallas kernels for 0% -> 0%
where the time goes in v1:
time: 200 us; the launch traced here: 199 us
  blocking collectives  98.2 us (49%)
  starting transfers between devices  35.8 us (18%)
  matrix products  19.1 us (10%)
  local copies, waits for them, and re-layouts  16.1 us (8%)
  between operations  14.4 us (7%)
  waiting for transfers between devices  10.4 us (5%)
  other arithmetic  5.34 us (3%)
    all_to_all x2, blocking collectives, local(): lax.all_to_all(sending, 'exp', split_axis=0, concat_axis=0, tiled=True)  63.9 us
    all_gather x2, blocking collectives, local(): full_hidden = lax.all_gather(hidden, 'hid', axis=2, tiled=True)  34.3 us
    all_to_all x2, starting transfers between devices, local(): lax.all_to_all(outgoing, 'exp', split_axis=0, concat_axis=0, tiled=True)  31.6 us
    all_to_all x2, waiting for transfers between devices, local(): lax.all_to_all(outgoing, 'exp', split_axis=0, concat_axis=0, tiled=True)  10.3 us
    all_to_all x4, local copies, waits for them, and re-layouts, local(): lax.all_to_all(outgoing, 'exp', split_axis=0, concat_axis=0, tiled=True)  6.58 us
    dot_general x4, matrix products, rotate(): jnp.einsum('...ab,ca,db->...cd', blocks, paley_table, sylvester_table, pr...  5.38 us
    dot_general x2, matrix products, local(): jnp.einsum('esd,efd->esf', expert_in, w_gate, preferred_element_type=jnp....  5.18 us
    all_to_all x1, starting transfers between devices, local(): lax.all_to_all(jnp.stack(jnp.split(w_down, lax.axis_size('hid'), axis=2))...  4.14 us
  transfers between devices with their start and end apart: 5, of which 1 were waited for; matrix products, arithmetic and copies ran while one was open for 13% of the time, Pallas kernels for 0%

profile of v1, /device:TPU:1, one launch (start us, length us, event | category | flops | bytes accessed | tf_op | source)
XLA Modules:
  0.0 199.3 jit_solution(7613712855650894384)
XLA Ops:
  7.2 0.0 all-gather.5.cloned.1.call-start
  7.2 0.9 fusion.82
  8.1 0.1 copy.26
  8.2 0.1 eq.58
  8.3 0.1 fusion.41
  8.4 0.2 reduce_window_sum.17
  8.5 0.2 select_reduce_fusion.1
  8.7 0.1 reshape.125
  8.8 0.1 fusion.38
  8.9 1.1 convolution_convert_fusion.3
  10.0 0.2 all_to_all.35
  10.3 37.8 %all_to_all.53 = bf16[128,2,1024]{2,1,0:T(2,128)(2,1)S(1)} all-to-all(bf16[128,2,1024]{2,1,0:T(2,128)(2,1)S(1)} %all_to_all.35), channel_id=1, replica_groups=mesh['exp'=128,'hid'=4] {'exp'}, dimensions={0} | all-to-all | bytes 1048576 | tf_op jit(solution)/shard_map/all_to_all | solution.py:80
  48.0 1.0 all_to_all.37
  49.1 0.0 all-gather.7.cloned.1.call-start
  49.1 0.1 copy.27
  49.2 0.1 eq.65
  49.3 0.1 fusion.40
  49.4 0.2 reduce_window_sum.18
  49.6 0.2 select_reduce_fusion
  49.7 0.1 reshape.130
  49.8 0.1 fusion.39
  50.0 0.3 convolution_convert_fusion.1
  50.3 0.2 all_to_all.42
  50.5 26.2 %all_to_all.54 = bf16[128,2,1024]{2,1,0:T(2,128)(2,1)S(1)} all-to-all(bf16[128,2,1024]{2,1,0:T(2,128)(2,1)S(1)} %all_to_all.42), channel_id=1, replica_groups=mesh['exp'=128,'hid'=4] {'exp'}, dimensions={0} | all-to-all | bytes 1048576 | tf_op jit(solution)/shard_map/all_to_all | solution.py:80
  76.7 1.0 all_to_all.44
  77.7 1.5 slice_bitcast_fusion.3
  79.2 1.4 pad_maximum_fusion
  80.6 4.1 %all-to-all-start.1 = ((bf16[4,1,192,1024]{3,2,1,0:T(8,128)(2,1)}), bf16[4,1,192,1024]{3,2,1,0:T(8,128)(2,1)S(1)}, u32[]{:S(2)}, u32[]{:S(2)}) async-start(bf16[4,1,192,1024]{3,2,1,0:T(8,128)(2,1)} %pad_maximum_fusion), calls=%async_computation.1 | async-start | bytes 3145728 | tf_op jit(solution)/shard_map/all_to_all | solution.py:63
  84.8 0.1 fusion.81
  84.8 0.1 reshape.142
  84.9 0.1 reshape.150
  85.0 0.7 copy.18
  85.7 0.7 copy.20
  86.4 0.6 convert_reduce_fusion
  87.0 2.6 %fusion.6 = f32[256,192]{0,1:T(8,128)S(1)} fusion(bf16[256,4096]{1,0:T(8,128)(2,1)} %all-gather.5.cloned.1.call-done, bf16[1,192,4096]{2,1,0:T(8,128)(2,1)S(1)} %copy-done), kind=kOutput, calls=%fused_computation.9 | convolution fusion | flops 402653184 | bytes 3866624 | tf_op jit(solution)/shard_map/esd,efd->esf/dot_general | solution.py:85
  89.6 0.1 copy-done.11
  89.6 0.8 fusion.20
  90.5 22.8 %all-gather = bf16[256,768]{0,1:T(8,128)(2,1)S(1)} all-gather(bf16[256,192]{0,1:T(8,128)(2,1)S(1)} %fusion.20), channel_id=2, replica_groups=mesh['exp'=128,'hid'=4] {'hid'}, dimensions={1}, use_global_device_ids=true | all-gather | bytes 491520 | tf_op jit(solution)/shard_map/all_gather | solution.py:88
  113.3 1.4 convolution_convert_fusion.2
  114.7 2.1 %all_to_all.39 = bf16[128,2,1024]{2,1,0:T(2,128)(2,1)} reshape(bf16[256,1024]{1,0:T(8,128)(2,1)} %convolution_convert_fusion.2) | data formatting | bytes 1048576 | tf_op jit(solution)/shard_map/all_to_all | solution.py:94
  116.8 16.1 %all-to-all-start.2 = ((bf16[128,2,1024]{2,1,0:T(2,128)(2,1)}), bf16[128,2,1024]{2,1,0:T(2,128)(2,1)}, u32[]{:S(2)}, u32[]{:S(2)}) async-start(bf16[128,2,1024]{2,1,0:T(2,128)(2,1)} %all_to_all.39), calls=%async_computation.2 | async-start | bytes 1048576 | tf_op jit(solution)/shard_map/all_to_all | solution.py:94
  132.8 0.0 all-gather.7.cloned.1.call-done
  132.9 2.6 %fusion.4 = f32[256,192]{0,1:T(8,128)S(1)} fusion(bf16[256,4096]{1,0:T(8,128)(2,1)} %all-gather.7.cloned.1.call-done, bf16[1,192,4096]{2,1,0:T(8,128)(2,1)S(1)} %copy-done), kind=kOutput, calls=%fused_computation.7 | convolution fusion | flops 402653184 | bytes 3866624 | tf_op jit(solution)/shard_map/esd,efd->esf/dot_general | solution.py:85
  135.5 0.0 copy-done.12
  135.5 0.9 fusion.17
  136.4 11.5 %all-gather.1 = bf16[256,768]{0,1:T(8,128)(2,1)S(1)} all-gather(bf16[256,192]{0,1:T(8,128)(2,1)S(1)} %fusion.17), channel_id=3, replica_groups=mesh['exp'=128,'hid'=4] {'hid'}, dimensions={1}, use_global_device_ids=true | all-gather | bytes 491520 | tf_op jit(solution)/shard_map/all_gather | solution.py:88
  147.8 0.8 copy-done.3
  148.6 1.4 convolution_convert_fusion
  150.0 2.0 %all_to_all.45 = bf16[128,2,1024]{2,1,0:T(2,128)(2,1)} reshape(bf16[256,1024]{1,0:T(8,128)(2,1)} %convolution_convert_fusion) | data formatting | bytes 1048576 | tf_op jit(solution)/shard_map/all_to_all | solution.py:94
  152.1 1.2 convert_multiply_fusion
  153.2 1.4 fusion.25
  154.6 15.5 %all-to-all-start.4 = ((bf16[128,2,1024]{2,1,0:T(2,128)(2,1)}), bf16[128,2,1024]{2,1,0:T(2,128)(2,1)}, u32[]{:S(2)}, u32[]{:S(2)}) async-start(bf16[128,2,1024]{2,1,0:T(2,128)(2,1)} %all_to_all.45), calls=%async_computation.4 | async-start | bytes 1048576 | tf_op jit(solution)/shard_map/all_to_all | solution.py:94
  170.2 1.3 fusion.29
  171.5 0.9 fusion.34
  172.4 1.4 fusion.23
  173.8 1.3 fusion.27
  175.1 1.7 fusion.10
  176.8 1.2 all_to_all.41
  178.1 0.9 gather_fusion
  178.9 10.3 %all-to-all-done.4 = bf16[128,2,1024]{2,1,0:T(2,128)(2,1)} async-done(((bf16[128,2,1024]{2,1,0:T(2,128)(2,1)}), bf16[128,2,1024]{2,1,0:T(2,128)(2,1)}, u32[]{:S(2)}, u32[]{:S(2)}) %all-to-all-start.4) | async-done | bytes 524320 | tf_op jit(solution)/shard_map/all_to_all | solution.py:94
  189.3 1.2 all_to_all.47
  190.5 0.9 gather_fusion.1
  191.4 0.4 fusion.31
  191.8 0.6 pad_maximum_fusion.1
  (33 shorter events, 0.2 us)
Async XLA Ops:
  7.2 79.8 %copy-start = (bf16[1,192,4096]{2,1,0:T(8,128)(2,1)S(1)}, bf16[1,192,4096]{2,1,0:T(8,128)(2,1)}, u32[]{:S(2)}) copy-start(bf16[1,192,4096]{2,1,0:T(8,128)(2,1)} %param.12) | copy-start | bytes 4718596
  7.2 79.8 %all-gather.5.cloned.1.call-start = ((), (), s32[]{:S(2)}) async-start(), calls=%async_computation.5 | async-start | bytes 2621440 | tf_op jit(solution)/shard_map/all_gather | solution.py:81
  10.3 39.7 %copy-start.4 = (bf16[32,1024]{1,0:T(8,128)(2,1)S(1)}, bf16[32,1024]{1,0:T(8,128)(2,1)}, u32[]{:S(2)}) copy-start(bf16[32,1024]{1,0:T(8,128)(2,1)} %param.8) | copy-start | bytes 196612
  49.1 83.8 %all-gather.7.cloned.1.call-start = ((), (), s32[]{:S(2)}) async-start(), calls=%async_computation.6 | async-start | bytes 2621440 | tf_op jit(solution)/shard_map/all_gather | solution.py:81
  80.6 4.2 %copy-start.9 = (f32[32,8]{0,1:T(8,128)S(1)}, f32[32,8]{0,1:T(8,128)}, u32[]{:S(2)}) copy-start(f32[32,8]{0,1:T(8,128)} %param.10) | copy-start | bytes 3076
  80.6 5.8 %copy-start.10 = (s32[1,768]{1,0:T(1,128)S(1)}, s32[1,768]{1,0:T(1,128)}, u32[]{:S(2)}) copy-start(s32[1,768]{1,0:T(1,128)} %param.11) | copy-start | bytes 9220
  80.6 32.7 %all-to-all-start.1 = ((bf16[4,1,192,1024]{3,2,1,0:T(8,128)(2,1)}), bf16[4,1,192,1024]{3,2,1,0:T(8,128)(2,1)S(1)}, u32[]{:S(2)}, u32[]{:S(2)}) async-start(bf16[4,1,192,1024]{3,2,1,0:T(8,128)(2,1)} %pad_maximum_fusion), calls=%async_computation.1 | async-start | bytes 3145728 | tf_op jit(solution)/shard_map/all_to_all | solution.py:63
  87.0 2.6 %copy-start.1 = (bf16[256,4096]{1,0:T(8,128)(2,1)S(1)}, bf16[256,4096]{1,0:T(8,128)(2,1)}, u32[]{:S(2)}) copy-start(bf16[256,4096]{1,0:T(8,128)(2,1)} %all-gather.5.cloned.1.call-done) | copy-start | bytes 6291460
  87.0 2.7 %copy-start.11 = (bf16[1,192,4096]{2,1,0:T(8,128)(2,1)S(1)}, bf16[1,192,4096]{2,1,0:T(8,128)(2,1)}, u32[]{:S(2)}) copy-start(bf16[1,192,4096]{2,1,0:T(8,128)(2,1)} %param.13) | copy-start | bytes 4718596
  116.8 37.9 %all-to-all-start.2 = ((bf16[128,2,1024]{2,1,0:T(2,128)(2,1)}), bf16[128,2,1024]{2,1,0:T(2,128)(2,1)}, u32[]{:S(2)}, u32[]{:S(2)}) async-start(bf16[128,2,1024]{2,1,0:T(2,128)(2,1)} %all_to_all.39), calls=%async_computation.2 | async-start | bytes 1048576 | tf_op jit(solution)/shard_map/all_to_all | solution.py:94
  132.8 2.6 %copy-start.2 = (bf16[256,4096]{1,0:T(8,128)(2,1)S(1)}, bf16[256,4096]{1,0:T(8,128)(2,1)}, u32[]{:S(2)}) copy-start(bf16[256,4096]{1,0:T(8,128)(2,1)} %all-gather.7.cloned.1.call-done) | copy-start | bytes 6291460
  132.9 2.7 %copy-start.12 = (bf16[1,192,4096]{2,1,0:T(8,128)(2,1)S(1)}, bf16[1,192,4096]{2,1,0:T(8,128)(2,1)}, u32[]{:S(2)}) copy-start(bf16[1,192,4096]{2,1,0:T(8,128)(2,1)} %param.13) | copy-start | bytes 4718596
  147.8 0.8 copy-start.3
  150.0 3.2 %copy-start.6 = (f32[12,12,1]{1,0,2:T(8,128)S(1)}, f32[12,12,1]{1,0,2:T(8,128)}, u32[]{:S(2)}) copy-start(f32[12,12,1]{1,0,2:T(8,128)} %constant.69) | copy-start | bytes 1732
  154.6 34.6 %all-to-all-start.4 = ((bf16[128,2,1024]{2,1,0:T(2,128)(2,1)}), bf16[128,2,1024]{2,1,0:T(2,128)(2,1)}, u32[]{:S(2)}, u32[]{:S(2)}) async-start(bf16[128,2,1024]{2,1,0:T(2,128)(2,1)} %all_to_all.45), calls=%async_computation.4 | async-start | bytes 1048576 | tf_op jit(solution)/shard_map/all_to_all | solution.py:94
  178.9 12.5 %copy-start.7 = (f32[16,8]{1,0:T(8,128)S(1)}, f32[16,8]{1,0:T(8,128)}, u32[]{:S(2)}) copy-start(f32[16,8]{1,0:T(8,128)} %copy.18) | copy-start | bytes 1540
  178.9 12.5 %copy-start.8 = (f32[16,8]{1,0:T(8,128)S(1)}, f32[16,8]{1,0:T(8,128)}, u32[]{:S(2)}) copy-start(f32[16,8]{1,0:T(8,128)} %copy.20) | copy-start | bytes 1540
  190.5 1.3 copy-start.5
Sparse Core Ops, SparseCore 0:
  49.2 29.5 all-gather.4
  80.9 45.0 all-gather.6
